TPU v7x, 256 devices: a whole 4x4x8 slice. The times are simulated.
256 devices in a mesh: tm: 4 (over y), row: 4 (over x), col: 16 (over z, core).
Axes of the slice: x: 4, y: 4, z: 8, core: 2. Of those that a mesh axis runs over, the one named last changes fastest.
Arguments:
- day_block: float32 [4, 4, 16, 32, 4, 4, 128], P('tm', None, 'col', None, None, 'row'), as said below
- left_coupling: float32 [4, 4, 16, 32, 4, 4, 128], P('tm', None, 'col', None, None, 'row'), may hold values from -0.125 to 0.125
- right_coupling: float32 [4, 4, 16, 32, 4, 4, 128], P('tm', None, 'col', None, None, 'row'), may hold values from -0.125 to 0.125
- separator_block: float32 [4, 4, 16, 32, 4, 4, 128], P('tm', None, 'col', None, None, 'row')
- arrow_coupling: float32 [4, 4, 16, 32, 64], P('tm', None, 'col'), may hold values from -0.125 to 0.125
- arrow_block: float32 [64, 64], replicated
Outputs:
- day_factor: float32 [4, 4, 16, 32, 4, 4, 128], P('tm', None, 'col', None, None, 'row')
- left_factor: float32 [4, 4, 16, 32, 4, 4, 128], P('tm', None, 'col', None, None, 'row')
- right_factor: float32 [4, 4, 16, 32, 4, 4, 128], P('tm', None, 'col', None, None, 'row')
- arrow_factor: float32 [4, 4, 16, 32, 64], P('tm', None, 'col')
- separator: float32 [4, 4, 16, 32, 4, 4, 128], P('tm', None, 'col', None, None, 'row')
- arrowhead: float32 [64, 64], replicated
Inputs may be any that keep to these rules, and one draw needn't show every extreme that they name: Each group's day_block and separator_block, and arrow_block, is an exactly symmetric matrix with all eigenvalues at least 1.
All inputs are finite; a program needn't handle non-finite values.
Results may differ from a plain program's by a relative error of at most 0.0001.
Values sent between devices are 32-bit elements; how exact they have to be, the bound alone decides.
No kernel may reach another device: no remote copies, remote signals or barrier semaphores. Data moves between devices by JAX's collectives and lax.ppermute only.
A program may use at most 128 MiB of HBM per device.

v0:
```python
import jax
import jax.numpy as jnp
from jax import lax
from jax.sharding import PartitionSpec as P


def passed_along(value, axis, steps):
    count = lax.axis_size(axis)
    initial, last = (max(0, -steps), min(count, count - steps))
    return lax.ppermute(value, axis, [(source, source + steps) for source in range(initial, last)])


def product(left, right):
    return jnp.dot(left, right, precision=lax.Precision.HIGHEST, preferred_element_type=jnp.float32)


def lower_inverse(factor):
    identity = jnp.eye(factor.shape[0], dtype=jnp.float32)
    return lax.linalg.triangular_solve(factor, identity, left_side=True, lower=True)


def reorder_nodes(whole, panels, col_width):
    count = whole.shape[0]
    col_count = lax.axis_size("col")
    spread = whole.reshape(count, panels, col_count, col_width)
    return jnp.transpose(spread, (2, 1, 3, 0)).reshape(col_count * panels * col_width, count)


def separator_term(solved, panels, col_width, row_width):
    whole = lax.all_gather(
        solved.reshape(solved.shape[0], panels, 1, row_width), "row", axis=2, tiled=True
    )
    ordered = reorder_nodes(whole, panels, col_width)
    return lax.psum_scatter(product(ordered, solved), "col", scatter_dimension=0, tiled=True)


def per_device(
    day_block, left_coupling, right_coupling, separator_block, arrow_coupling, arrow_block
):
    panels = day_block.shape[1]
    col_width = day_block.shape[3]
    row_width = day_block.shape[6]
    panel_size = col_width * lax.axis_size("col")
    arrow_rows = arrow_block.shape[0]
    col_index = lax.axis_index("col")
    row_index = lax.axis_index("row")
    matrix = day_block.reshape(panels, col_width, panels, row_width)
    left_part = left_coupling.reshape(panels, col_width, panels, row_width)
    right_part = right_coupling.reshape(panels, col_width, panels, row_width)
    arrow_part = arrow_coupling.reshape(panels, col_width, arrow_rows)
    rows_at = col_index * col_width + lax.broadcasted_iota(jnp.int32, (col_width, row_width), 0)
    cols_at = row_index * row_width + lax.broadcasted_iota(jnp.int32, (col_width, row_width), 1)
    factor_blocks = []
    left_blocks = []
    right_blocks = []
    arrow_blocks = []
    for current in range(panels):
        remain = panels - current
        gathered_day, gathered_left, gathered_right, gathered_arrow = (
            lax.all_gather(matrix[current, :, current:, :], "col", axis=0, tiled=True),
            lax.all_gather(left_part[current], "col", axis=0, tiled=True),
            lax.all_gather(right_part[current], "col", axis=0, tiled=True),
            lax.all_gather(arrow_part[current], "col", axis=0, tiled=True),
        )
        diagonal_full = lax.all_gather(gathered_day[:, 0:1, :], "row", axis=1, tiled=True).reshape(
            panel_size, panel_size
        )
        factor = jnp.linalg.cholesky(diagonal_full)
        inverse = lower_inverse(factor)
        owned = product(inverse, gathered_day.reshape(panel_size, remain * row_width)).reshape(
            panel_size, remain, row_width
        )
        if remain > 1:
            later = lax.all_gather(owned[:, 1:, None, :], "row", axis=2, tiled=True).reshape(
                panel_size, remain - 1, panel_size
            )
        solved_left = product(inverse, gathered_left.reshape(panel_size, panels * row_width))
        solved_right = product(inverse, gathered_right.reshape(panel_size, panels * row_width))
        solved_arrow = product(inverse, gathered_arrow)
        mine_rows = lax.dynamic_slice_in_dim(owned, col_index * col_width, col_width, 0)
        diagonal_part = jnp.where(cols_at >= rows_at, mine_rows[:, 0, :], 0.0)
        factor_blocks.append(
            jnp.concatenate(
                [
                    jnp.zeros((col_width, current, row_width), jnp.float32),
                    diagonal_part[:, None, :],
                    mine_rows[:, 1:, :],
                ],
                axis=1,
            )
        )
        left_blocks.append(
            lax.dynamic_slice_in_dim(solved_left, col_index * col_width, col_width, 0)
        )
        right_blocks.append(
            lax.dynamic_slice_in_dim(solved_right, col_index * col_width, col_width, 0)
        )
        arrow_blocks.append(
            lax.dynamic_slice_in_dim(solved_arrow, col_index * col_width, col_width, 0)
        )
        if remain > 1:
            mine_later = lax.dynamic_slice_in_dim(later, col_index * col_width, col_width, 2)
            mine_later = mine_later.reshape(panel_size, (remain - 1) * col_width).T
            owned_later = owned[:, 1:, :].reshape(panel_size, (remain - 1) * row_width)
            matrix = matrix.at[current + 1 :, :, current + 1 :, :].add(
                -product(mine_later, owned_later).reshape(
                    remain - 1, col_width, remain - 1, row_width
                )
            )
            left_part = left_part.at[current + 1 :].add(
                -product(mine_later, solved_left).reshape(remain - 1, col_width, panels, row_width)
            )
            right_part = right_part.at[current + 1 :].add(
                -product(mine_later, solved_right).reshape(remain - 1, col_width, panels, row_width)
            )
            arrow_part = arrow_part.at[current + 1 :].add(
                -product(mine_later, solved_arrow).reshape(remain - 1, col_width, arrow_rows)
            )
    day_factor = jnp.stack(factor_blocks).reshape(day_block.shape)
    left_solved = jnp.stack(left_blocks).reshape(panels * col_width, panels * row_width)
    right_solved = jnp.stack(right_blocks).reshape(panels * col_width, panels * row_width)
    arrow_solved = jnp.stack(arrow_blocks).reshape(panels * col_width, arrow_rows)
    separator_local = separator_block.reshape(panels * col_width, panels * row_width)
    right_term = separator_term(right_solved, panels, col_width, row_width)
    left_term = separator_term(left_solved, panels, col_width, row_width)
    from_next = passed_along(left_term, "tm", -1)
    separator = separator_local - right_term - from_next
    arrow_local = product(arrow_solved.T, arrow_solved)
    arrow_local = jnp.where(row_index == 0, arrow_local, 0.0)
    arrow_total = lax.psum(arrow_local, ("tm", "row", "col"))
    arrowhead = arrow_block - arrow_total
    return (
        day_factor,
        left_solved.reshape(left_coupling.shape),
        right_solved.reshape(right_coupling.shape),
        arrow_solved.reshape(arrow_coupling.shape),
        separator.reshape(separator_block.shape),
        arrowhead,
    )


def solution(mesh):
    return jax.shard_map(
        per_device,
        mesh=mesh,
        in_specs=(
            P("tm", None, "col", None, None, "row", None),
            P("tm", None, "col", None, None, "row", None),
            P("tm", None, "col", None, None, "row", None),
            P("tm", None, "col", None, None, "row", None),
            P("tm", None, "col", None, None),
            P(),
        ),
        out_specs=(
            P("tm", None, "col", None, None, "row", None),
            P("tm", None, "col", None, None, "row", None),
            P("tm", None, "col", None, None, "row", None),
            P("tm", None, "col", None, None),
            P("tm", None, "col", None, None, "row", None),
            P(),
        ),
        check_vma=False,
    )
```

profile of v0, /device:TPU:1, one launch (start us, length us, event | category | flops | bytes accessed | tf_op | source)
XLA Modules:
  0.0 1345.4 jit_solution(15966232665213219999)
XLA Ops:
  8.8 44.4 %all-gather.49.cloned.1.call-done = f32[1,1,1,512,4,1,128]{6,4,5,2,1,0,3:T(4,128)} async-done(((f32[1,1,1,32,4,1,128]{6,4,5,2,1,0,3:T(4,128)}), f32[1,1,1,512,4,1,128]{6,4,5,2,1,0,3:T(4,128)}) %all-gather.49.cloned.1.call-update) | async-done | bytes 1048592 | tf_op jit(solution)/shard_map/all_gather | solution.py:60
  58.0 20.3 %all-gather.39.cloned.1.call-done = f32[512,4,128]{2,0,1:T(8,128)} async-done(((f32[512,1,128]{2,0,1:T(8,128)}), f32[512,4,128]{2,0,1:T(8,128)}) %all-gather.39.cloned.1.call-update) | async-done | bytes 1048592 | tf_op jit(solution)/shard_map/all_gather | solution.py:65
  81.4 11.7 cholesky.462
  105.6 11.7 cholesky.481
  117.3 10.2 custom-call.36
  129.2 11.7 cholesky.502
  152.8 11.9 cholesky.519
  176.8 39.3 %custom-call.38 = f32[4,128,128]{1,2,0:T(8,128)S(1)} custom-call(f32[4,128,128]{2,1,0:T(8,128)S(1)} %get-tuple-element.178), custom_call_target="InvertDiagBlocksLowerTriangular" | custom-call | tf_op jit(solution)/shard_map/triangular_solve/custom-call.3 | solution.py:19
  227.9 44.9 %all-gather.51.cloned.1.call-done = f32[512,3,512]{2,0,1:T(8,128)} async-done(((f32[512,3,128]{2,0,1:T(8,128)}), f32[512,3,512]{2,0,1:T(8,128)}) %all-gather.51.cloned.1.call-update) | async-done | bytes 3145744 | tf_op jit(solution)/shard_map/all_gather | solution.py:74
  278.0 21.4 %all-gather.2 = f32[1,512,3,128]{3,1,2,0:T(8,128)S(1)} all-gather(f32[1,32,3,128]{3,1,2,0:T(8,128)S(1)} %slice.678), channel_id=4, replica_groups=mesh['tm'=4,'row'=4,'col'=16] {'col'}, dimensions={1}, use_global_device_ids=true | all-gather | bytes 835584 | tf_op jit(solution)/shard_map/all_gather | solution.py:60
  301.6 21.1 %all-gather.41.cloned.1.call-done = f32[512,4,128]{2,0,1:T(8,128)} async-done(((f32[512,1,128]{2,0,1:T(8,128)}), f32[512,4,128]{2,0,1:T(8,128)}) %all-gather.41.cloned.1.call-update) | async-done | bytes 1048592 | tf_op jit(solution)/shard_map/all_gather | solution.py:65
  328.0 11.7 cholesky.534
  352.8 11.7 cholesky.553
  377.0 11.7 cholesky.574
  400.6 11.9 cholesky.591
  417.0 11.6 while.21
  428.6 39.3 %custom-call.42 = f32[4,128,128]{1,2,0:T(8,128)S(1)} custom-call(f32[4,128,128]{2,1,0:T(8,128)S(1)} %get-tuple-element.179), custom_call_target="InvertDiagBlocksLowerTriangular" | custom-call | tf_op jit(solution)/shard_map/triangular_solve/custom-call.3 | solution.py:19
  485.3 32.5 %all-gather.53.cloned.1.call-done = f32[512,2,512]{2,0,1:T(8,128)} async-done(((f32[512,2,128]{2,0,1:T(8,128)}), f32[512,2,512]{2,0,1:T(8,128)}) %all-gather.53.cloned.1.call-update) | async-done | bytes 2097168 | tf_op jit(solution)/shard_map/all_gather | solution.py:74
  522.9 20.8 %all-gather.4 = f32[1,512,2,128]{3,1,2,0:T(8,128)S(1)} all-gather(f32[1,32,2,128]{3,1,2,0:T(8,128)S(1)} %slice.689), channel_id=6, replica_groups=mesh['tm'=4,'row'=4,'col'=16] {'col'}, dimensions={1}, use_global_device_ids=true | all-gather | bytes 557056 | tf_op jit(solution)/shard_map/all_gather | solution.py:60
  545.3 16.1 %all-gather.59.cloned.1.call-done = f32[1,1,1,512,4,1,128]{6,4,5,2,1,0,3:T(4,128)} async-done(((f32[1,1,1,32,4,1,128]{6,4,5,2,1,0,3:T(4,128)}), f32[1,1,1,512,4,1,128]{6,4,5,2,1,0,3:T(4,128)}) %all-gather.59.cloned.1.call-update) | async-done | bytes 1048592 | tf_op jit(solution)/shard_map/all_gather | solution.py:61
  572.7 27.8 %all-gather.67.cloned.1.call-done = f32[1,1,1,512,4,1,128]{6,4,5,2,1,0,3:T(4,128)} async-done(((f32[1,1,1,32,4,1,128]{6,4,5,2,1,0,3:T(4,128)}), f32[1,1,1,512,4,1,128]{6,4,5,2,1,0,3:T(4,128)}) %all-gather.67.cloned.1.call-update) | async-done | bytes 1048592 | tf_op jit(solution)/shard_map/all_gather | solution.py:62
  612.0 13.6 %all-gather.43.cloned.1.call-done = f32[512,4,128]{2,0,1:T(8,128)} async-done(((f32[512,1,128]{2,0,1:T(8,128)}), f32[512,4,128]{2,0,1:T(8,128)}) %all-gather.43.cloned.1.call-update) | async-done | bytes 1048592 | tf_op jit(solution)/shard_map/all_gather | solution.py:65
  630.8 11.7 cholesky.606
  656.4 11.7 cholesky.625
  681.2 11.7 cholesky.646
  704.9 11.9 cholesky.663
  721.1 11.5 while.22
  732.6 39.3 %custom-call.46 = f32[4,128,128]{1,2,0:T(8,128)S(1)} custom-call(f32[4,128,128]{2,1,0:T(8,128)S(1)} %get-tuple-element.180), custom_call_target="InvertDiagBlocksLowerTriangular" | custom-call | tf_op jit(solution)/shard_map/triangular_solve/custom-call.3 | solution.py:19
  815.0 22.1 %all-gather.6 = f32[1,512,1,128]{3,1,2,0:T(8,128)} all-gather(f32[1,32,1,128]{3,1,2,0:T(8,128)S(1)} %fusion.16), channel_id=8, replica_groups=mesh['tm'=4,'row'=4,'col'=16] {'col'}, dimensions={1}, use_global_device_ids=true | all-gather | bytes 278528 | tf_op jit(solution)/shard_map/all_gather | solution.py:60
  837.2 17.1 %all-gather.63.cloned.1.call-done = f32[1,512,4,128]{3,1,2,0:T(8,128)} async-done(((f32[1,32,4,128]{3,1,2,0:T(8,128)}), f32[1,512,4,128]{3,1,2,0:T(8,128)}) %all-gather.63.cloned.1.call-update) | async-done | bytes 1048592 | tf_op jit(solution)/shard_map/all_gather | solution.py:61
  869.4 24.0 %all-gather.71.cloned.1.call-done = f32[1,512,4,128]{3,1,2,0:T(8,128)} async-done(((f32[1,32,4,128]{3,1,2,0:T(8,128)}), f32[1,512,4,128]{3,1,2,0:T(8,128)}) %all-gather.71.cloned.1.call-update) | async-done | bytes 1048592 | tf_op jit(solution)/shard_map/all_gather | solution.py:62
  905.8 12.0 all-gather.57.cloned.1.call-done
  923.0 11.7 cholesky.678
  935.4 10.4 custom-call.47
  950.6 13.2 cholesky.697
  966.0 11.5 custom-call.48
  981.2 13.2 cholesky.718
  996.5 11.3 custom-call.49
  1010.8 13.6 %cholesky.735 = f32[128,128]{1,0:T(8,128)} custom-call(f32[128,128]{1,0:T(8,128)} %convolution_subtract_fusion.20), custom_call_target="Cholesky" | custom-call | tf_op jit(solution)/shard_map/jit(cholesky)/cholesky | solution.py:68
  1029.5 11.6 while.23
  1041.1 39.3 %custom-call.50 = f32[4,128,128]{1,2,0:T(8,128)S(1)} custom-call(f32[4,128,128]{2,1,0:T(8,128)S(1)} %get-tuple-element.181), custom_call_target="InvertDiagBlocksLowerTriangular" | custom-call | tf_op jit(solution)/shard_map/triangular_solve/custom-call.3 | solution.py:19
  1105.2 16.4 %all-gather.47.cloned.1.call-done = f32[128,4,4,128]{3,0,1,2:T(8,128)} async-done(((f32[128,4,1,128]{3,0,1,2:T(8,128)}), f32[128,4,4,128]{3,0,1,2:T(8,128)}) %all-gather.47.cloned.1.call-update) | async-done | bytes 1048592 | tf_op jit(solution)/shard_map/all_gather | solution.py:30
  1128.5 21.8 %all-gather.45.cloned.1.call-done = f32[128,4,4,128]{3,0,1,2:T(8,128)} async-done(((f32[128,4,1,128]{3,0,1,2:T(8,128)}), f32[128,4,4,128]{3,0,1,2:T(8,128)}) %all-gather.45.cloned.1.call-update) | async-done | bytes 1048592 | tf_op jit(solution)/shard_map/all_gather | solution.py:30
  1157.6 20.8 %all-gather.16 = f32[1,1,1,512,64]{4,3,2,1,0:T(8,128)S(1)} all-gather(f32[1,1,1,32,64]{4,3,2,1,0:T(8,128)S(1)} %slice-done.1), channel_id=18, replica_groups=mesh['tm'=4,'row'=4,'col'=16] {'col'}, dimensions={3}, use_global_device_ids=true | all-gather | bytes 139264 | tf_op jit(solution)/shard_map/all_gather | solution.py:63
  1187.4 15.8 %all-gather.17 = f32[1,512,64]{2,1,0:T(8,128)S(1)} all-gather(f32[1,32,64]{2,1,0:T(8,128)S(1)} %slice.716), channel_id=19, replica_groups=mesh['tm'=4,'row'=4,'col'=16] {'col'}, dimensions={1}, use_global_device_ids=true | all-gather | bytes 139264 | tf_op jit(solution)/shard_map/all_gather | solution.py:63
  1208.7 16.2 %all-gather.18 = f32[1,512,64]{2,1,0:T(8,128)S(1)} all-gather(f32[1,32,64]{2,1,0:T(8,128)S(1)} %slice.718), channel_id=20, replica_groups=mesh['tm'=4,'row'=4,'col'=16] {'col'}, dimensions={1}, use_global_device_ids=true | all-gather | bytes 139264 | tf_op jit(solution)/shard_map/all_gather | solution.py:63
  1230.8 16.0 %all-gather.19 = f32[1,512,64]{2,1,0:T(8,128)S(1)} all-gather(f32[1,32,64]{2,1,0:T(8,128)S(1)} %fusion.14), channel_id=21, replica_groups=mesh['tm'=4,'row'=4,'col'=16] {'col'}, dimensions={1}, use_global_device_ids=true | all-gather | bytes 139264 | tf_op jit(solution)/shard_map/all_gather | solution.py:63
  1250.3 74.9 %psum.7 = f32[64,64]{1,0:T(8,128)S(1)} all-reduce(f32[64,64]{1,0:T(8,128)S(1)} %fusion.12), channel_id=1, replica_groups=mesh['tm'=4,'row'=4,'col'=16] {'tm','row','col'}, use_global_device_ids=true, to_apply=%region_10.0 | all-reduce | flops 4096 | bytes 32768 | tf_op jit(solution)/shard_map/psum | solution.py:130
  (494 shorter events, 413.1 us)
Async XLA Ops:
  7.2 46.0 %all-gather.49.cloned.1.call-start = ((), (), s32[]{:S(2)}) async-start(), calls=%async_computation.9 | async-start | bytes 1114112 | tf_op jit(solution)/shard_map/all_gather | solution.py:60
  8.7 69.5 %all-gather.39.cloned.1.call-start = ((), (), s32[]{:S(2)}) async-start(), calls=%async_computation.2 | async-start | bytes 1310720 | tf_op jit(solution)/shard_map/all_gather | solution.py:65
  55.3 217.5 %all-gather.51.cloned.1.call-start = ((), (), s32[]{:S(2)}) async-start(), calls=%async_computation.10 | async-start | bytes 3932160 | tf_op jit(solution)/shard_map/all_gather | solution.py:74
  219.1 381.4 %copy-start = (f32[128,512]{1,0:T(8,128)}, f32[128,512]{1,0:T(8,128)S(1)}, u32[]{:S(2)}) copy-start(f32[128,512]{1,0:T(8,128)S(1)} %fusion.152) | copy-start | bytes 786436
  221.2 53.9 %copy-start.11 = (f32[128,512]{1,0:T(8,128)}, f32[128,512]{1,0:T(8,128)S(1)}, u32[]{:S(2)}) copy-start(f32[128,512]{1,0:T(8,128)S(1)} %fusion.151) | copy-start | bytes 786436
  226.3 96.4 %all-gather.41.cloned.1.call-start = ((), (), s32[]{:S(2)}) async-start(), calls=%async_computation.3 | async-start | bytes 1310720 | tf_op jit(solution)/shard_map/all_gather | solution.py:65
  276.4 329.7 %copy-start.9 = (f32[512,3,32]{0,2,1:T(8,128)}, f32[512,3,32]{0,2,1:T(8,128)S(1)}, u32[]{:S(2)}) copy-start(f32[512,3,32]{0,2,1:T(8,128)S(1)} %copy.124) | copy-start | bytes 589828
  300.2 217.7 %all-gather.53.cloned.1.call-start = ((), (), s32[]{:S(2)}) async-start(), calls=%async_computation.11 | async-start | bytes 2621440 | tf_op jit(solution)/shard_map/all_gather | solution.py:74
  471.8 48.2 %copy-start.2 = (f32[128,512]{1,0:T(8,128)}, f32[128,512]{1,0:T(8,128)S(1)}, u32[]{:S(2)}) copy-start(f32[128,512]{1,0:T(8,128)S(1)} %fusion.146) | copy-start | bytes 786436
  479.3 82.1 %copy-start.12 = (f32[128,512]{1,0:T(8,128)S(1)}, f32[128,512]{1,0:T(8,128)}, u32[]{:S(2)}) copy-start(f32[128,512]{1,0:T(8,128)} %copy-done.11) | copy-start | bytes 786436
  480.1 81.3 %all-gather.59.cloned.1.call-start = ((), (), s32[]{:S(2)}) async-start(), calls=%async_computation.14 | async-start | bytes 1114112 | tf_op jit(solution)/shard_map/all_gather | solution.py:61
  481.7 118.8 %all-gather.67.cloned.1.call-start = ((), (), s32[]{:S(2)}) async-start(), calls=%async_computation.18 | async-start | bytes 1114112 | tf_op jit(solution)/shard_map/all_gather | solution.py:62
  483.2 142.4 %all-gather.43.cloned.1.call-start = ((), (), s32[]{:S(2)}) async-start(), calls=%async_computation.4 | async-start | bytes 1310720 | tf_op jit(solution)/shard_map/all_gather | solution.py:65
  519.9 48.1 %slice-start = ((f32[1,4,1,32,4,1,128]{6,5,4,3,2,1,0:T(1,128)}), f32[1,3,1,32,4,1,128]{6,5,4,3,2,1,0:T(1,128)S(1)}, s32[]{:S(2)}) async-start(f32[1,4,1,32,4,1,128]{6,5,4,3,2,1,0:T(1,128)} %param.34), calls=%async_computation.22 | async-start | bytes 393216 | tf_op jit(solution)/shard_map/slice.420
  522.8 47.5 %copy-start.57 = (f32[2,32,2,128]{3,1,2,0:T(8,128)}, f32[2,32,2,128]{3,1,2,0:T(8,128)S(1)}, u32[]{:S(2)}) copy-start(f32[2,32,2,128]{3,1,2,0:T(8,128)S(1)} %fusion.9) | copy-start | bytes 196612
  545.2 238.8 %all-gather.61.cloned.1.call-start = ((), (), s32[]{:S(2)}) async-start(), calls=%async_computation.15 | async-start | bytes 1114112 | tf_op jit(solution)/shard_map/all_gather | solution.py:61
  571.1 226.4 %all-gather.69.cloned.1.call-start = ((), (), s32[]{:S(2)}) async-start(), calls=%async_computation.19 | async-start | bytes 1114112 | tf_op jit(solution)/shard_map/all_gather | solution.py:62
  609.5 201.7 %all-gather.55.cloned.1.call-start = ((), (), s32[]{:S(2)}) async-start(), calls=%async_computation.12 | async-start | bytes 1310720 | tf_op jit(solution)/shard_map/all_gather | solution.py:74
  774.0 121.9 %copy-start.5 = (f32[128,512]{1,0:T(8,128)}, f32[128,512]{1,0:T(8,128)S(1)}, u32[]{:S(2)}) copy-start(f32[128,512]{1,0:T(8,128)S(1)} %fusion.142) | copy-start | bytes 786436
  776.8 119.1 %copy-start.17 = (f32[128,512]{1,0:T(8,128)}, f32[128,512]{1,0:T(8,128)S(1)}, u32[]{:S(2)}) copy-start(f32[128,512]{1,0:T(8,128)S(1)} %fusion.140) | copy-start | bytes 786436
  784.0 70.3 %all-gather.63.cloned.1.call-start = ((), (), s32[]{:S(2)}) async-start(), calls=%async_computation.16 | async-start | bytes 1114112 | tf_op jit(solution)/shard_map/all_gather | solution.py:61
  796.9 96.4 %all-gather.71.cloned.1.call-start = ((), (), s32[]{:S(2)}) async-start(), calls=%async_computation.20 | async-start | bytes 1114112 | tf_op jit(solution)/shard_map/all_gather | solution.py:62
  804.0 52.8 %copy-start.29 = (f32[128,512]{1,0:T(8,128)S(1)}, f32[128,512]{1,0:T(8,128)}, u32[]{:S(2)}) copy-start(f32[128,512]{1,0:T(8,128)} %copy-done.28) | copy-start | bytes 786436
  809.0 51.9 %copy-start.45 = (f32[2,32,4,128]{3,1,2,0:T(8,128)}, f32[2,32,4,128]{3,1,2,0:T(8,128)S(1)}, u32[]{:S(2)}) copy-start(f32[2,32,4,128]{3,1,2,0:T(8,128)S(1)} %fusion.3) | copy-start | bytes 393220
  809.7 108.1 %all-gather.57.cloned.1.call-start = ((), (), s32[]{:S(2)}) async-start(), calls=%async_computation.13 | async-start | bytes 1310720 | tf_op jit(solution)/shard_map/all_gather | solution.py:65
  813.7 49.7 %copy-start.47 = (f32[2,32,4,128]{3,1,2,0:T(8,128)S(1)}, f32[2,32,4,128]{3,1,2,0:T(8,128)}, u32[]{:S(2)}) copy-start(f32[2,32,4,128]{3,1,2,0:T(8,128)} %copy-done.46) | copy-start | bytes 393220
  837.1 251.1 %all-gather.65.cloned.1.call-start = ((), (), s32[]{:S(2)}) async-start(), calls=%async_computation.17 | async-start | bytes 1114112 | tf_op jit(solution)/shard_map/all_gather | solution.py:61
  866.4 232.6 %all-gather.73.cloned.1.call-start = ((), (), s32[]{:S(2)}) async-start(), calls=%async_computation.21 | async-start | bytes 1114112 | tf_op jit(solution)/shard_map/all_gather | solution.py:62
  905.6 216.0 %all-gather.47.cloned.1.call-start = ((), (), s32[]{:S(2)}) async-start(), calls=%async_computation.7 | async-start | bytes 1310720 | tf_op jit(solution)/shard_map/all_gather | solution.py:30
  1094.5 55.9 %all-gather.45.cloned.1.call-start = ((), (), s32[]{:S(2)}) async-start(), calls=%async_computation.5 | async-start | bytes 1310720 | tf_op jit(solution)/shard_map/all_gather | solution.py:30
  1105.2 222.1 %reduce-scatter.5.cloned.1.call-start = ((), (), s32[]{:S(2)}) async-start(), calls=%async_computation.8 | async-start | bytes 4456448 | tf_op jit(solution)/shard_map/reduce_scatter | solution.py:34
  1128.3 203.2 %reduce-scatter.3.cloned.1.call-start = ((), (), s32[]{:S(2)}) async-start(), calls=%async_computation.6 | async-start | bytes 4456448 | tf_op jit(solution)/shard_map/reduce_scatter | solution.py:34
  1157.0 46.1 %copy-start.4 = (f32[128,512]{1,0:T(8,128)S(1)}, f32[128,512]{1,0:T(8,128)}, u32[]{:S(2)}) copy-start(f32[128,512]{1,0:T(8,128)} %copy-done.2) | copy-start | bytes 786436
  1157.0 46.1 %copy-start.16 = (f32[128,512]{1,0:T(8,128)S(1)}, f32[128,512]{1,0:T(8,128)}, u32[]{:S(2)}) copy-start(f32[128,512]{1,0:T(8,128)} %copy-done.14) | copy-start | bytes 786436
  1157.1 67.8 %copy-start.6 = (f32[128,512]{1,0:T(8,128)S(1)}, f32[128,512]{1,0:T(8,128)}, u32[]{:S(2)}) copy-start(f32[128,512]{1,0:T(8,128)} %copy-done.5) | copy-start | bytes 786436
  1157.1 67.8 %copy-start.18 = (f32[128,512]{1,0:T(8,128)S(1)}, f32[128,512]{1,0:T(8,128)}, u32[]{:S(2)}) copy-start(f32[128,512]{1,0:T(8,128)} %copy-done.17) | copy-start | bytes 786436
  1181.4 43.6 %copy-start.30 = (f32[128,512]{1,0:T(8,128)S(1)}, f32[128,512]{1,0:T(8,128)}, u32[]{:S(2)}) copy-start(f32[128,512]{1,0:T(8,128)} %copy-done.28) | copy-start | bytes 786436
  1181.4 65.5 %copy-start.8 = (f32[128,512]{1,0:T(8,128)S(1)}, f32[128,512]{1,0:T(8,128)}, u32[]{:S(2)}) copy-start(f32[128,512]{1,0:T(8,128)} %copy-done.7) | copy-start | bytes 786436
  1181.4 65.5 %copy-start.20 = (f32[128,512]{1,0:T(8,128)S(1)}, f32[128,512]{1,0:T(8,128)}, u32[]{:S(2)}) copy-start(f32[128,512]{1,0:T(8,128)} %copy-done.19) | copy-start | bytes 786436
  1181.4 65.5 %copy-start.32 = (f32[128,512]{1,0:T(8,128)S(1)}, f32[128,512]{1,0:T(8,128)}, u32[]{:S(2)}) copy-start(f32[128,512]{1,0:T(8,128)} %copy-done.31) | copy-start | bytes 786436
  1204.3 42.6 %copy-start.38 = (f32[1,512,1,128]{3,1,2,0:T(8,128)S(1)}, f32[1,512,1,128]{3,1,2,0:T(8,128)}, u32[]{:S(2)}) copy-start(f32[1,512,1,128]{3,1,2,0:T(8,128)} %all-gather.6) | copy-start | bytes 786436
  1204.3 43.6 %copy-start.62 = (s32[32]{0:T(128)S(1)}, s32[32]{0:T(128)}, u32[]{:S(2)}) copy-start(s32[32]{0:T(128)} %iota_add_fusion) | copy-start | bytes 388
  1204.3 43.6 %copy-start.63 = (s32[128]{0:T(128)S(1)}, s32[128]{0:T(128)}, u32[]{:S(2)}) copy-start(s32[128]{0:T(128)} %iota_add_fusion.1) | copy-start | bytes 1540
  1224.9 100.3 %copy-start.61 = (f32[64,64]{1,0:T(8,128)S(1)}, f32[64,64]{1,0:T(8,128)}, u32[]{:S(2)}) copy-start(f32[64,64]{1,0:T(8,128)} %param.38) | copy-start | bytes 49156
  1226.1 103.5 %copy-start.55 = (f32[1,1,1,32,4,1,128]{6,5,4,3,2,1,0:T(1,128)S(1)}, f32[1,1,1,32,4,1,128]{6,5,4,3,2,1,0:T(1,128)}, u32[]{:S(2)}) copy-start(f32[1,1,1,32,4,1,128]{6,5,4,3,2,1,0:T(1,128)} %stack.85) | copy-start | bytes 196612
  1226.1 104.5 %copy-start.54 = (f32[1,1,1,32,4,1,128]{6,5,4,3,2,1,0:T(1,128)S(1)}, f32[1,1,1,32,4,1,128]{6,5,4,3,2,1,0:T(1,128)}, u32[]{:S(2)}) copy-start(f32[1,1,1,32,4,1,128]{6,5,4,3,2,1,0:T(1,128)} %stack.90) | copy-start | bytes 196612
  1227.1 109.5 %copy-start.53 = (f32[1,4,1,32,4,1,128]{6,5,4,3,2,1,0:T(1,128)S(1)}, f32[1,4,1,32,4,1,128]{6,5,4,3,2,1,0:T(1,128)}, u32[]{:S(2)}) copy-start(f32[1,4,1,32,4,1,128]{6,5,4,3,2,1,0:T(1,128)} %param.36) | copy-start | bytes 786436
  1327.3 9.3 collective-permute-start
  (39 other events, 315.4 us)
Sparse Core Ops, SparseCore 0:
  10.4 42.7 all-gather.48
  55.5 22.6 all-gather.38
  226.5 46.2 all-gather.50
  300.3 22.3 all-gather.40
  480.3 37.5 all-gather.52
  520.1 41.2 all-gather.58
  563.2 37.2 all-gather.66
  602.9 22.6 all-gather.42
  627.5 41.9 all-gather.60
  671.1 37.1 all-gather.68
  784.1 26.9 all-gather.54
  812.9 41.3 all-gather.62
  856.1 37.2 all-gather.70
  895.0 22.7 all-gather.56
  919.5 41.7 all-gather.64
  963.0 37.2 all-gather.72
  1094.6 26.9 all-gather.46
  1123.3 27.0 all-gather.44
  1152.9 63.7 reduce-scatter.4
  1219.1 62.5 reduce-scatter.2
where the time goes:
time: 1360 us; the launch traced here: 1350 us
  other arithmetic  503 us (37%)
  waiting for transfers between devices  319 us (23%)
  blocking collectives  208 us (15%)
  local copies, waits for them, and re-layouts  159 us (12%)
  matrix products  126 us (9%)
  between operations  26.5 us (2%)
    another operation x59, other arithmetic, per_device(): factor = jnp.linalg.cholesky(diagonal_full)  329 us
    another operation x9, other arithmetic, lower_inverse(): lax.linalg.triangular_solve(factor, identity, left_side=True, lower=True)  161 us
    all_gather x3, waiting for transfers between devices, per_device(): lax.all_gather(owned[:, 1:, None, :], 'row', axis=2, tiled=True)  78.9 us
    psum x1, blocking collectives, per_device(): arrow_total = lax.psum(arrow_local, ('tm', 'row', 'col'))  74.9 us
    dot_general x31, matrix products, product(): jnp.dot(left, right, precision=lax.Precision.HIGHEST, preferred_element_t...  73.6 us
    all_gather x4, blocking collectives, per_device(): lax.all_gather(arrow_part[current], 'col', axis=0, tiled=True)  68.8 us
    all_gather x4, waiting for transfers between devices, per_device(): lax.all_gather(gathered_day[:, 0:1, :], 'row', axis=1, tiled=True)  66.9 us
    all_gather x3, blocking collectives, per_device(): lax.all_gather(matrix[current, :, current:, :], 'col', axis=0, tiled=True)  64.4 us
  transfers between devices with their start and end apart: 21, of which 15 were waited for; matrix products, arithmetic and copies ran while one was open for 35% of the time, Pallas kernels for 0%

commit v1 on v0

--- a/solution.py
+++ b/solution.py
@@ -1,7 +1,20 @@
+import functools
 import jax
 import jax.numpy as jnp
 from jax import lax
 from jax.sharding import PartitionSpec as P
+
+
+def push_array(row_data, axis_key):
+    return jnp.concatenate(
+        jax.lax.all_to_all(
+            jnp.stack([row_data for _ in range(jax.lax.axis_size(axis_key))]), axis_key, 0, 0
+        ),
+        axis=0,
+    )
+
+
+perform_arrays = functools.partial(push_array, axis_key="col")
 
 
 def passed_along(value, axis, steps):
@@ -58,7 +71,7 @@
         remain = panels - current
         gathered_day, gathered_left, gathered_right, gathered_arrow = (
             lax.all_gather(matrix[current, :, current:, :], "col", axis=0, tiled=True),
-            lax.all_gather(left_part[current], "col", axis=0, tiled=True),
+            perform_arrays(left_part[current]),
             lax.all_gather(right_part[current], "col", axis=0, tiled=True),
             lax.all_gather(arrow_part[current], "col", axis=0, tiled=True),
         )

time: 1360 us -> 1290 us (0.949)
  waiting for transfers between devices: 319 us -> 208 us
  starting transfers between devices: 3.49 us -> 32.6 us
  blocking collectives: 208 us -> 225 us
    all_gather x4, waiting for transfers between devices: 51.8 us -> 8.54 us  [per_device(): lax.all_gather(right_part[current], 'col', axis=0, tiled=True)]
    all_gather x4 -> x0, waiting for transfers between devices: 33.3 us -> none  [per_device(): lax.all_gather(left_part[current], 'col', axis=0, tiled=True)]
    all_to_all x0 -> x4, starting transfers between devices: none -> 29.5 us  [push_array(): jax.lax.all_to_all(jnp.stack([row_data for _ in range(jax.lax.axis_size(a...]
    all_gather x4, waiting for transfers between devices: 66.9 us -> 44.7 us  [per_device(): lax.all_gather(gathered_day[:, 0:1, :], 'row', axis=1, tiled=True)]
    all_gather x3, blocking collectives: 64.4 us -> 80.8 us  [per_device(): lax.all_gather(matrix[current, :, current:, :], 'col', axis=0, tiled=True)]
  transfers between devices with their start and end apart: 21 -> 21, of which waited for: 15 -> 10; matrix products, arithmetic and copies ran while one was open for 35% -> 36% of each run, Pallas kernels for 0% -> 0%
where the time goes in v1:
time: 1290 us; the launch traced here: 1280 us
  other arithmetic  503 us (39%)
  blocking collectives  225 us (17%)
  waiting for transfers between devices  208 us (16%)
  local copies, waits for them, and re-layouts  154 us (12%)
  matrix products  127 us (10%)
  starting transfers between devices  32.6 us (3%)
  between operations  26.2 us (2%)
    another operation x59, other arithmetic, per_device(): factor = jnp.linalg.cholesky(diagonal_full)  329 us
    another operation x9, other arithmetic, lower_inverse(): lax.linalg.triangular_solve(factor, identity, left_side=True, lower=True)  161 us
    all_gather x3, blocking collectives, per_device(): lax.all_gather(matrix[current, :, current:, :], 'col', axis=0, tiled=True)  80.8 us
    psum x1, blocking collectives, per_device(): arrow_total = lax.psum(arrow_local, ('tm', 'row', 'col'))  75 us
    dot_general x31, matrix products, product(): jnp.dot(left, right, precision=lax.Precision.HIGHEST, preferred_element_t...  74.3 us
    all_gather x3, waiting for transfers between devices, per_device(): lax.all_gather(owned[:, 1:, None, :], 'row', axis=2, tiled=True)  69 us
    all_gather x4, blocking collectives, per_device(): lax.all_gather(arrow_part[current], 'col', axis=0, tiled=True)  68.8 us
    all_gather x4, waiting for transfers between devices, per_device(): lax.all_gather(gathered_day[:, 0:1, :], 'row', axis=1, tiled=True)  44.7 us
  transfers between devices with their start and end apart: 21, of which 10 were waited for; matrix products, arithmetic and copies ran while one was open for 36% of the time, Pallas kernels for 0%

profile of v1, /device:TPU:1, one launch (start us, length us, event | category | flops | bytes accessed | tf_op | source)
XLA Modules:
  0.0 1275.8 jit_solution(15707889670963329472)
XLA Ops:
  8.8 44.4 %all-gather.41.cloned.1.call-done = f32[1,1,1,512,4,1,128]{6,4,5,2,1,0,3:T(4,128)} async-done(((f32[1,1,1,32,4,1,128]{6,4,5,2,1,0,3:T(4,128)}), f32[1,1,1,512,4,1,128]{6,4,5,2,1,0,3:T(4,128)}) %all-gather.41.cloned.1.call-update) | async-done | bytes 1048592 | tf_op jit(solution)/shard_map/all_gather | solution.py:73
  58.0 20.3 %all-gather.31.cloned.1.call-done = f32[512,4,128]{2,0,1:T(8,128)} async-done(((f32[512,1,128]{2,0,1:T(8,128)}), f32[512,4,128]{2,0,1:T(8,128)}) %all-gather.31.cloned.1.call-update) | async-done | bytes 1048592 | tf_op jit(solution)/shard_map/all_gather | solution.py:78
  81.4 11.7 cholesky.462
  93.1 9.8 custom-call.35
  105.6 11.7 cholesky.481
  117.4 10.2 custom-call.36
  129.2 11.7 cholesky.502
  141.6 9.8 custom-call.37
  152.8 11.9 cholesky.519
  176.8 39.3 %custom-call.38 = f32[4,128,128]{1,2,0:T(8,128)S(1)} custom-call(f32[4,128,128]{2,1,0:T(8,128)S(1)} %get-tuple-element.178), custom_call_target="InvertDiagBlocksLowerTriangular" | custom-call | tf_op jit(solution)/shard_map/triangular_solve/custom-call.3 | solution.py:32
  227.9 44.9 %all-gather.43.cloned.1.call-done = f32[512,3,512]{2,0,1:T(8,128)} async-done(((f32[512,3,128]{2,0,1:T(8,128)}), f32[512,3,512]{2,0,1:T(8,128)}) %all-gather.43.cloned.1.call-update) | async-done | bytes 3145744 | tf_op jit(solution)/shard_map/all_gather | solution.py:87
  278.0 21.4 %all-gather.2 = f32[1,512,3,128]{3,1,2,0:T(8,128)S(1)} all-gather(f32[1,32,3,128]{3,1,2,0:T(8,128)S(1)} %slice.690), channel_id=4, replica_groups=mesh['tm'=4,'row'=4,'col'=16] {'col'}, dimensions={1}, use_global_device_ids=true | all-gather | bytes 835584 | tf_op jit(solution)/shard_map/all_gather | solution.py:73
  301.6 21.1 %all-gather.33.cloned.1.call-done = f32[512,4,128]{2,0,1:T(8,128)} async-done(((f32[512,1,128]{2,0,1:T(8,128)}), f32[512,4,128]{2,0,1:T(8,128)}) %all-gather.33.cloned.1.call-update) | async-done | bytes 1048592 | tf_op jit(solution)/shard_map/all_gather | solution.py:78
  328.0 11.7 cholesky.534
  352.8 11.7 cholesky.553
  365.2 10.2 custom-call.40
  377.0 11.7 cholesky.574
  389.4 9.8 custom-call.41
  400.7 11.9 cholesky.591
  417.0 11.6 while.21
  428.5 39.3 %custom-call.42 = f32[4,128,128]{1,2,0:T(8,128)S(1)} custom-call(f32[4,128,128]{2,1,0:T(8,128)S(1)} %get-tuple-element.179), custom_call_target="InvertDiagBlocksLowerTriangular" | custom-call | tf_op jit(solution)/shard_map/triangular_solve/custom-call.3 | solution.py:32
  493.1 24.1 %all-gather.45.cloned.1.call-done = f32[512,2,512]{2,0,1:T(8,128)} async-done(((f32[512,2,128]{2,0,1:T(8,128)}), f32[512,2,512]{2,0,1:T(8,128)}) %all-gather.45.cloned.1.call-update) | async-done | bytes 2097168 | tf_op jit(solution)/shard_map/all_gather | solution.py:87
  520.3 20.7 %all-gather.4 = f32[1,512,2,128]{3,1,2,0:T(8,128)S(1)} all-gather(f32[1,32,2,128]{3,1,2,0:T(8,128)S(1)} %slice.701), channel_id=6, replica_groups=mesh['tm'=4,'row'=4,'col'=16] {'col'}, dimensions={1}, use_global_device_ids=true | all-gather | bytes 557056 | tf_op jit(solution)/shard_map/all_gather | solution.py:73
  590.9 11.7 cholesky.606
  603.4 9.8 custom-call.43
  616.5 11.7 cholesky.625
  629.0 10.0 custom-call.44
  641.4 11.7 cholesky.646
  665.0 11.9 cholesky.663
  681.3 12.0 while.22
  693.4 39.3 %custom-call.46 = f32[4,128,128]{1,2,0:T(8,128)S(1)} custom-call(f32[4,128,128]{2,1,0:T(8,128)S(1)} %get-tuple-element.180), custom_call_target="InvertDiagBlocksLowerTriangular" | custom-call | tf_op jit(solution)/shard_map/triangular_solve/custom-call.3 | solution.py:32
  781.5 38.6 %all-gather.6 = f32[1,512,1,128]{3,1,2,0:T(8,128)} all-gather(f32[1,32,1,128]{3,1,2,0:T(8,128)S(1)} %fusion.17), channel_id=8, replica_groups=mesh['tm'=4,'row'=4,'col'=16] {'col'}, dimensions={1}, use_global_device_ids=true | all-gather | bytes 278528 | tf_op jit(solution)/shard_map/all_gather | solution.py:73
  856.7 11.7 cholesky.678
  869.1 10.4 custom-call.47
  884.3 13.2 %cholesky.697 = f32[128,128]{1,0:T(8,128)} custom-call(f32[128,128]{1,0:T(8,128)} %cholesky.789), custom_call_target="Cholesky" | custom-call | tf_op jit(solution)/shard_map/jit(cholesky)/cholesky | solution.py:81
  899.7 11.5 custom-call.48
  914.9 13.2 %cholesky.718 = f32[128,128]{1,0:T(8,128)} custom-call(f32[128,128]{1,0:T(8,128)} %cholesky.794), custom_call_target="Cholesky" | custom-call | tf_op jit(solution)/shard_map/jit(cholesky)/cholesky | solution.py:81
  930.2 11.3 custom-call.49
  944.4 13.6 %cholesky.735 = f32[128,128]{1,0:T(8,128)} custom-call(f32[128,128]{1,0:T(8,128)} %convolution_subtract_fusion.20), custom_call_target="Cholesky" | custom-call | tf_op jit(solution)/shard_map/jit(cholesky)/cholesky | solution.py:81
  963.2 11.6 while.23
  974.7 39.3 %custom-call.50 = f32[4,128,128]{1,2,0:T(8,128)S(1)} custom-call(f32[4,128,128]{2,1,0:T(8,128)S(1)} %get-tuple-element.181), custom_call_target="InvertDiagBlocksLowerTriangular" | custom-call | tf_op jit(solution)/shard_map/triangular_solve/custom-call.3 | solution.py:32
  1038.5 13.6 %all-gather.39.cloned.1.call-done = f32[128,4,4,128]{3,0,1,2:T(8,128)} async-done(((f32[128,4,1,128]{3,0,1,2:T(8,128)}), f32[128,4,4,128]{3,0,1,2:T(8,128)}) %all-gather.39.cloned.1.call-update) | async-done | bytes 1048592 | tf_op jit(solution)/shard_map/all_gather | solution.py:43
  1059.0 21.8 %all-gather.37.cloned.1.call-done = f32[128,4,4,128]{3,0,1,2:T(8,128)} async-done(((f32[128,4,1,128]{3,0,1,2:T(8,128)}), f32[128,4,4,128]{3,0,1,2:T(8,128)}) %all-gather.37.cloned.1.call-update) | async-done | bytes 1048592 | tf_op jit(solution)/shard_map/all_gather | solution.py:43
  1088.1 20.9 %all-gather.12 = f32[1,1,1,512,64]{4,3,2,1,0:T(8,128)S(1)} all-gather(f32[1,1,1,32,64]{4,3,2,1,0:T(8,128)S(1)} %slice-done.1), channel_id=14, replica_groups=mesh['tm'=4,'row'=4,'col'=16] {'col'}, dimensions={3}, use_global_device_ids=true | all-gather | bytes 139264 | tf_op jit(solution)/shard_map/all_gather | solution.py:76
  1118.0 15.7 %all-gather.13 = f32[1,512,64]{2,1,0:T(8,128)S(1)} all-gather(f32[1,32,64]{2,1,0:T(8,128)S(1)} %slice.728), channel_id=15, replica_groups=mesh['tm'=4,'row'=4,'col'=16] {'col'}, dimensions={1}, use_global_device_ids=true | all-gather | bytes 139264 | tf_op jit(solution)/shard_map/all_gather | solution.py:76
  1139.3 16.5 %all-gather.14 = f32[1,512,64]{2,1,0:T(8,128)S(1)} all-gather(f32[1,32,64]{2,1,0:T(8,128)S(1)} %slice.730), channel_id=16, replica_groups=mesh['tm'=4,'row'=4,'col'=16] {'col'}, dimensions={1}, use_global_device_ids=true | all-gather | bytes 139264 | tf_op jit(solution)/shard_map/all_gather | solution.py:76
  1161.7 15.8 %all-gather.15 = f32[1,512,64]{2,1,0:T(8,128)S(1)} all-gather(f32[1,32,64]{2,1,0:T(8,128)S(1)} %fusion.15), channel_id=17, replica_groups=mesh['tm'=4,'row'=4,'col'=16] {'col'}, dimensions={1}, use_global_device_ids=true | all-gather | bytes 139264 | tf_op jit(solution)/shard_map/all_gather | solution.py:76
  1180.9 75.0 %psum.7 = f32[64,64]{1,0:T(8,128)S(1)} all-reduce(f32[64,64]{1,0:T(8,128)S(1)} %fusion.13), channel_id=1, replica_groups=mesh['tm'=4,'row'=4,'col'=16] {'tm','row','col'}, use_global_device_ids=true, to_apply=%region_10.0 | all-reduce | flops 4096 | bytes 32768 | tf_op jit(solution)/shard_map/psum | solution.py:143
  (496 shorter events, 389.7 us)
Async XLA Ops:
  7.2 46.0 %all-gather.41.cloned.1.call-start = ((), (), s32[]{:S(2)}) async-start(), calls=%async_computation.13 | async-start | bytes 1114112 | tf_op jit(solution)/shard_map/all_gather | solution.py:73
  8.7 69.5 %all-gather.31.cloned.1.call-start = ((), (), s32[]{:S(2)}) async-start(), calls=%async_computation.6 | async-start | bytes 1310720 | tf_op jit(solution)/shard_map/all_gather | solution.py:78
  55.3 217.5 %all-gather.43.cloned.1.call-start = ((), (), s32[]{:S(2)}) async-start(), calls=%async_computation.14 | async-start | bytes 3932160 | tf_op jit(solution)/shard_map/all_gather | solution.py:87
  176.8 39.8 %copy-start.25 = (f32[512,512]{1,0:T(8,128)}, f32[512,512]{1,0:T(8,128)S(1)}, u32[]{:S(2)}) copy-start(f32[512,512]{1,0:T(8,128)S(1)} %get-tuple-element.505) | copy-start | bytes 3145732
  219.1 341.1 %copy-start = (f32[128,512]{1,0:T(8,128)}, f32[128,512]{1,0:T(8,128)S(1)}, u32[]{:S(2)}) copy-start(f32[128,512]{1,0:T(8,128)S(1)} %fusion.162) | copy-start | bytes 786436
  221.2 53.9 %copy-start.12 = (f32[128,512]{1,0:T(8,128)}, f32[128,512]{1,0:T(8,128)S(1)}, u32[]{:S(2)}) copy-start(f32[128,512]{1,0:T(8,128)S(1)} %fusion.161) | copy-start | bytes 786436
  226.4 96.3 %all-gather.33.cloned.1.call-start = ((), (), s32[]{:S(2)}) async-start(), calls=%async_computation.7 | async-start | bytes 1310720 | tf_op jit(solution)/shard_map/all_gather | solution.py:78
  276.5 294.1 %copy-start.9 = (f32[512,3,32]{0,2,1:T(8,128)}, f32[512,3,32]{0,2,1:T(8,128)S(1)}, u32[]{:S(2)}) copy-start(f32[512,3,32]{0,2,1:T(8,128)S(1)} %copy.127) | copy-start | bytes 589828
  300.2 217.1 %all-gather.45.cloned.1.call-start = ((), (), s32[]{:S(2)}) async-start(), calls=%async_computation.15 | async-start | bytes 2621440 | tf_op jit(solution)/shard_map/all_gather | solution.py:87
  479.5 80.7 %all-gather.51.cloned.1.call-start = ((), (), s32[]{:S(2)}) async-start(), calls=%async_computation.18 | async-start | bytes 1114112 | tf_op jit(solution)/shard_map/all_gather | solution.py:75
  482.3 62.8 %all-to-all-start = ((f32[16,32,4,128]{3,2,1,0:T(4,128)}), f32[16,32,4,128]{3,2,1,0:T(4,128)}, u32[]{:S(2)}, u32[]{:S(2)}) async-start(f32[16,32,4,128]{3,2,1,0:T(4,128)} %stack.97), calls=%async_computation | async-start | bytes 2097152 | tf_op jit(solution)/shard_map/all_to_all | solution.py:10
  492.1 53.0 %copy-start.13 = (f32[128,512]{1,0:T(8,128)S(1)}, f32[128,512]{1,0:T(8,128)}, u32[]{:S(2)}) copy-start(f32[128,512]{1,0:T(8,128)} %copy-done.12) | copy-start | bytes 786436
  492.1 93.6 %all-gather.35.cloned.1.call-start = ((), (), s32[]{:S(2)}) async-start(), calls=%async_computation.8 | async-start | bytes 1310720 | tf_op jit(solution)/shard_map/all_gather | solution.py:78
  520.3 44.0 %copy-start.58 = (f32[2,32,2,128]{3,1,2,0:T(8,128)}, f32[2,32,2,128]{3,1,2,0:T(8,128)S(1)}, u32[]{:S(2)}) copy-start(f32[2,32,2,128]{3,1,2,0:T(8,128)S(1)} %fusion.10) | copy-start | bytes 196612
  574.6 183.4 %all-to-all-start.1 = ((f32[16,32,4,128]{3,2,1,0:T(4,128)}), f32[16,32,4,128]{3,2,1,0:T(4,128)}, u32[]{:S(2)}, u32[]{:S(2)}) async-start(f32[16,32,4,128]{3,2,1,0:T(4,128)} %stack.99), calls=%async_computation.1 | async-start | bytes 2097152 | tf_op jit(solution)/shard_map/all_to_all | solution.py:10
  579.1 166.0 %all-gather.53.cloned.1.call-start = ((), (), s32[]{:S(2)}) async-start(), calls=%async_computation.19 | async-start | bytes 1114112 | tf_op jit(solution)/shard_map/all_gather | solution.py:75
  579.9 197.9 %all-gather.47.cloned.1.call-start = ((), (), s32[]{:S(2)}) async-start(), calls=%async_computation.16 | async-start | bytes 1310720 | tf_op jit(solution)/shard_map/all_gather | solution.py:87
  734.8 97.6 %copy-start.5 = (f32[128,512]{1,0:T(8,128)}, f32[128,512]{1,0:T(8,128)S(1)}, u32[]{:S(2)}) copy-start(f32[128,512]{1,0:T(8,128)S(1)} %fusion.152) | copy-start | bytes 786436
  737.5 94.8 %copy-start.18 = (f32[128,512]{1,0:T(8,128)}, f32[128,512]{1,0:T(8,128)S(1)}, u32[]{:S(2)}) copy-start(f32[128,512]{1,0:T(8,128)S(1)} %fusion.150) | copy-start | bytes 786436
  744.8 85.0 %all-gather.55.cloned.1.call-start = ((), (), s32[]{:S(2)}) async-start(), calls=%async_computation.20 | async-start | bytes 1114112 | tf_op jit(solution)/shard_map/all_gather | solution.py:75
  764.6 58.5 %copy-start.31 = (f32[128,512]{1,0:T(8,128)S(1)}, f32[128,512]{1,0:T(8,128)}, u32[]{:S(2)}) copy-start(f32[128,512]{1,0:T(8,128)} %copy-done.30) | copy-start | bytes 786436
  767.0 60.2 %copy-start.48 = (f32[2,32,4,128]{3,1,2,0:T(8,128)}, f32[2,32,4,128]{3,1,2,0:T(8,128)S(1)}, u32[]{:S(2)}) copy-start(f32[2,32,4,128]{3,1,2,0:T(8,128)S(1)} %fusion.4) | copy-start | bytes 393220
  768.3 54.9 %all-to-all-start.2 = ((f32[16,32,4,128]{3,2,1,0:T(4,128)}), f32[16,32,4,128]{3,2,1,0:T(4,128)}, u32[]{:S(2)}, u32[]{:S(2)}) async-start(f32[16,32,4,128]{3,2,1,0:T(4,128)} %stack.101), calls=%async_computation.2 | async-start | bytes 2097152 | tf_op jit(solution)/shard_map/all_to_all | solution.py:10
  777.7 73.8 %all-gather.49.cloned.1.call-start = ((), (), s32[]{:S(2)}) async-start(), calls=%async_computation.17 | async-start | bytes 1310720 | tf_op jit(solution)/shard_map/all_gather | solution.py:78
  842.9 178.9 %all-to-all-start.3 = ((f32[16,32,4,128]{3,2,1,0:T(4,128)}), f32[16,32,4,128]{3,2,1,0:T(4,128)}, u32[]{:S(2)}, u32[]{:S(2)}) async-start(f32[16,32,4,128]{3,2,1,0:T(4,128)} %stack.103), calls=%async_computation.3 | async-start | bytes 2097152 | tf_op jit(solution)/shard_map/all_to_all | solution.py:10
  848.6 183.6 %all-gather.57.cloned.1.call-start = ((), (), s32[]{:S(2)}) async-start(), calls=%async_computation.21 | async-start | bytes 1114112 | tf_op jit(solution)/shard_map/all_gather | solution.py:75
  851.2 200.9 %all-gather.39.cloned.1.call-start = ((), (), s32[]{:S(2)}) async-start(), calls=%async_computation.11 | async-start | bytes 1310720 | tf_op jit(solution)/shard_map/all_gather | solution.py:43
  1027.8 53.1 %all-gather.37.cloned.1.call-start = ((), (), s32[]{:S(2)}) async-start(), calls=%async_computation.9 | async-start | bytes 1310720 | tf_op jit(solution)/shard_map/all_gather | solution.py:43
  1038.4 219.5 %reduce-scatter.5.cloned.1.call-start = ((), (), s32[]{:S(2)}) async-start(), calls=%async_computation.12 | async-start | bytes 4456448 | tf_op jit(solution)/shard_map/reduce_scatter | solution.py:47
  1058.8 203.4 %reduce-scatter.3.cloned.1.call-start = ((), (), s32[]{:S(2)}) async-start(), calls=%async_computation.10 | async-start | bytes 4456448 | tf_op jit(solution)/shard_map/reduce_scatter | solution.py:47
  1082.5 27.6 %copy-start.1 = (f32[128,512]{1,0:T(8,128)S(1)}, f32[128,512]{1,0:T(8,128)}, u32[]{:S(2)}) copy-start(f32[128,512]{1,0:T(8,128)} %copy-done) | copy-start | bytes 786436
  1087.5 28.6 %copy-start.10 = (f32[512,3,32]{0,2,1:T(8,128)S(1)}, f32[512,3,32]{0,2,1:T(8,128)}, u32[]{:S(2)}) copy-start(f32[512,3,32]{0,2,1:T(8,128)} %copy-done.9) | copy-start | bytes 589828
  1087.5 46.1 %copy-start.4 = (f32[128,512]{1,0:T(8,128)S(1)}, f32[128,512]{1,0:T(8,128)}, u32[]{:S(2)}) copy-start(f32[128,512]{1,0:T(8,128)} %copy-done.2) | copy-start | bytes 786436
  1087.5 46.1 %copy-start.17 = (f32[128,512]{1,0:T(8,128)S(1)}, f32[128,512]{1,0:T(8,128)}, u32[]{:S(2)}) copy-start(f32[128,512]{1,0:T(8,128)} %copy-done.15) | copy-start | bytes 786436
  1087.6 68.2 %copy-start.6 = (f32[128,512]{1,0:T(8,128)S(1)}, f32[128,512]{1,0:T(8,128)}, u32[]{:S(2)}) copy-start(f32[128,512]{1,0:T(8,128)} %copy-done.5) | copy-start | bytes 786436
  1087.6 68.2 %copy-start.19 = (f32[128,512]{1,0:T(8,128)S(1)}, f32[128,512]{1,0:T(8,128)}, u32[]{:S(2)}) copy-start(f32[128,512]{1,0:T(8,128)} %copy-done.18) | copy-start | bytes 786436
  1112.0 43.8 %copy-start.32 = (f32[128,512]{1,0:T(8,128)S(1)}, f32[128,512]{1,0:T(8,128)}, u32[]{:S(2)}) copy-start(f32[128,512]{1,0:T(8,128)} %copy-done.30) | copy-start | bytes 786436
  1112.0 65.5 %copy-start.8 = (f32[128,512]{1,0:T(8,128)S(1)}, f32[128,512]{1,0:T(8,128)}, u32[]{:S(2)}) copy-start(f32[128,512]{1,0:T(8,128)} %copy-done.7) | copy-start | bytes 786436
  1112.0 65.5 %copy-start.21 = (f32[128,512]{1,0:T(8,128)S(1)}, f32[128,512]{1,0:T(8,128)}, u32[]{:S(2)}) copy-start(f32[128,512]{1,0:T(8,128)} %copy-done.20) | copy-start | bytes 786436
  1112.0 65.5 %copy-start.34 = (f32[128,512]{1,0:T(8,128)S(1)}, f32[128,512]{1,0:T(8,128)}, u32[]{:S(2)}) copy-start(f32[128,512]{1,0:T(8,128)} %copy-done.33) | copy-start | bytes 786436
  1134.8 42.6 %copy-start.40 = (f32[1,512,1,128]{3,1,2,0:T(8,128)S(1)}, f32[1,512,1,128]{3,1,2,0:T(8,128)}, u32[]{:S(2)}) copy-start(f32[1,512,1,128]{3,1,2,0:T(8,128)} %all-gather.6) | copy-start | bytes 786436
  1134.8 43.6 %copy-start.63 = (s32[32]{0:T(128)S(1)}, s32[32]{0:T(128)}, u32[]{:S(2)}) copy-start(s32[32]{0:T(128)} %iota_add_fusion) | copy-start | bytes 388
  1134.8 43.6 %copy-start.64 = (s32[128]{0:T(128)S(1)}, s32[128]{0:T(128)}, u32[]{:S(2)}) copy-start(s32[128]{0:T(128)} %iota_add_fusion.1) | copy-start | bytes 1540
  1155.8 100.1 %copy-start.62 = (f32[64,64]{1,0:T(8,128)S(1)}, f32[64,64]{1,0:T(8,128)}, u32[]{:S(2)}) copy-start(f32[64,64]{1,0:T(8,128)} %param.38) | copy-start | bytes 49156
  1156.9 103.4 %copy-start.56 = (f32[1,1,1,32,4,1,128]{6,5,4,3,2,1,0:T(1,128)S(1)}, f32[1,1,1,32,4,1,128]{6,5,4,3,2,1,0:T(1,128)}, u32[]{:S(2)}) copy-start(f32[1,1,1,32,4,1,128]{6,5,4,3,2,1,0:T(1,128)} %stack.98) | copy-start | bytes 196612
  1156.9 104.3 %copy-start.55 = (f32[1,1,1,32,4,1,128]{6,5,4,3,2,1,0:T(1,128)S(1)}, f32[1,1,1,32,4,1,128]{6,5,4,3,2,1,0:T(1,128)}, u32[]{:S(2)}) copy-start(f32[1,1,1,32,4,1,128]{6,5,4,3,2,1,0:T(1,128)} %stack.106) | copy-start | bytes 196612
  1158.0 109.3 %copy-start.54 = (f32[1,4,1,32,4,1,128]{6,5,4,3,2,1,0:T(1,128)S(1)}, f32[1,4,1,32,4,1,128]{6,5,4,3,2,1,0:T(1,128)}, u32[]{:S(2)}) copy-start(f32[1,4,1,32,4,1,128]{6,5,4,3,2,1,0:T(1,128)} %param.36) | copy-start | bytes 786436
  1258.0 9.3 collective-permute-start
  (40 other events, 246.9 us)
Sparse Core Ops, SparseCore 0:
  10.4 42.7 all-gather.40
  55.5 22.6 all-gather.30
  226.5 46.2 all-gather.42
  300.3 22.3 all-gather.32
  479.6 37.5 all-gather.44
  518.9 41.2 all-gather.50
  562.6 22.9 all-gather.34
  587.5 41.6 all-gather.52
  744.9 26.7 all-gather.46
  773.4 45.2 all-gather.54
  820.5 22.5 all-gather.48
  851.4 40.5 all-gather.56
  1027.9 24.2 all-gather.38
  1053.8 27.0 all-gather.36
  1083.2 63.9 reduce-scatter.4
  1149.6 62.5 reduce-scatter.2
